TPU v7x, 128 devices: a whole 4x4x4 slice. The times are simulated.
128 devices in a mesh: expert: 16 (over y, x), etp: 8 (over z, core).
Axes of the slice: x: 4, y: 4, z: 4, core: 2. Of those that a mesh axis runs over, the one named last changes fastest.
Arguments:
- tokens: bfloat16 [2048, 2048], P('expert'), may hold values from -6 to 6
- out_grad: bfloat16 [2048, 2048], P('expert'), may hold values from -6 to 6
- routes: int32 [2048, 2], P('expert'), may hold values from 0 to 15, as said below
- combine_weights: float32 [2048, 2], P('expert'), may hold values from 0.2 to 1
- w_gate: bfloat16 [16, 2048, 7168], P('expert', None, 'etp'), may hold values from -0.125 to 0.125
- w_up: bfloat16 [16, 2048, 7168], P('expert', None, 'etp'), may hold values from -0.125 to 0.125
- w_down: bfloat16 [16, 7168, 2048], P('expert', 'etp'), may hold values from -0.0625 to 0.0625
Outputs:
- mixed: bfloat16 [2048, 2048], P('expert')
- tokens_grad: bfloat16 [2048, 2048], P('expert')
- combine_grad: float32 [2048, 2], P('expert')
- gate_weight_grad: bfloat16 [16, 2048, 7168], P('expert', None, 'etp')
- up_weight_grad: bfloat16 [16, 2048, 7168], P('expert', None, 'etp')
- down_weight_grad: bfloat16 [16, 7168, 2048], P('expert', 'etp')
Inputs may be any that keep to these rules, and one draw needn't show every extreme that they name: `routes`: each token names two different experts. No expert is named by more than 32 tokens of one group of 128 consecutive tokens, and one expert, the same in every group, is named by exactly 32 tokens of each group.
All inputs are finite; a program needn't handle non-finite values.
Results may differ from a plain program's by a relative error of at most 0.02.
Values may be sent and summed in bfloat16 or wider, within the bound.
No kernel may reach another device: no remote copies, remote signals or barrier semaphores. Data moves between devices by JAX's collectives and lax.ppermute only.
A program may use at most 128 MiB of HBM per device.

v0:
```python
import jax
import jax.numpy as jnp
from jax import lax
from jax.sharding import PartitionSpec as P

TOP = 2


def slot_numbers(routes, expert_count):
    flattened = routes.reshape(-1)
    one_hot = (flattened[:, None] == jnp.arange(expert_count, dtype=jnp.int32)[None, :]).astype(
        jnp.int32
    )
    before = jnp.cumsum(one_hot, axis=0) - one_hot
    return jnp.sum(before * one_hot, axis=1).reshape(routes.shape)


def contract_last(left, right):
    return lax.dot_general(
        left, right, (((1,), (1,)), ((), ())), preferred_element_type=jnp.float32
    )


def contract_first(left, right):
    return lax.dot_general(
        left, right, (((0,), (0,)), ((), ())), preferred_element_type=jnp.float32
    )


def expert_pass(rows_in, rows_grad, gate_w, up_w, down_w):
    gate_pre = jnp.dot(rows_in, gate_w, preferred_element_type=jnp.float32)
    up_pre = jnp.dot(rows_in, up_w, preferred_element_type=jnp.float32)
    gate_sig = jax.nn.sigmoid(gate_pre)
    swish = gate_pre * gate_sig
    hidden = (swish * up_pre).astype(jnp.bfloat16)
    out_part = jnp.dot(hidden, down_w, preferred_element_type=jnp.float32)
    hidden_grad = contract_last(rows_grad, down_w)
    down_grad = contract_first(hidden, rows_grad).astype(jnp.bfloat16)
    gate_grad = (hidden_grad * up_pre * gate_sig * (1.0 + gate_pre * (1.0 - gate_sig))).astype(
        jnp.bfloat16
    )
    up_grad = (hidden_grad * swish).astype(jnp.bfloat16)
    gate_weight_grad = contract_first(rows_in, gate_grad).astype(jnp.bfloat16)
    up_weight_grad = contract_first(rows_in, up_grad).astype(jnp.bfloat16)
    input_part = contract_last(gate_grad, gate_w) + contract_last(up_grad, up_w)
    return (out_part, input_part, gate_weight_grad, up_weight_grad, down_grad)


def shards(tokens, out_grad, routes, combine_weights, w_gate, w_up, w_down):
    expert_count = lax.axis_size("expert")
    token_count, features = tokens.shape
    capacity = token_count // 4
    slots = slot_numbers(routes, expert_count)
    position = routes * capacity + slots
    pair_count = token_count * TOP
    source_index = jnp.full((expert_count * capacity,), pair_count, jnp.int32)
    source_index = source_index.at[position.reshape(-1)].set(
        jnp.arange(pair_count, dtype=jnp.int32)
    )
    zero_row = jnp.zeros((1, features), jnp.bfloat16)
    padded_tokens = jnp.concatenate([tokens, zero_row], axis=0)
    scaled_grad = (combine_weights[:, :, None] * out_grad[:, None, :]).astype(jnp.bfloat16)
    padded_grad = jnp.concatenate([scaled_grad.reshape(pair_count, features), zero_row], axis=0)
    send_rows = padded_tokens[source_index // TOP].reshape(expert_count, capacity, features)
    send_grad = padded_grad[source_index].reshape(expert_count, capacity, features)
    recv_rows, recv_grad = (
        lax.all_to_all(send_rows, "expert", split_axis=0, concat_axis=0, tiled=True),
        lax.all_to_all(send_grad, "expert", split_axis=0, concat_axis=0, tiled=True),
    )
    rows_in = recv_rows.reshape(expert_count * capacity, features)
    rows_grad = recv_grad.reshape(expert_count * capacity, features)
    out_part, input_part, gate_weight_grad, up_weight_grad, down_weight_grad = expert_pass(
        rows_in, rows_grad, w_gate[0], w_up[0], w_down[0]
    )
    out_part = out_part.reshape(expert_count, capacity, features)
    input_part = input_part.reshape(expert_count, capacity, features)
    grad_values = out_grad.astype(jnp.float32)
    out_sum, input_sum = (
        lax.psum(out_part.astype(jnp.bfloat16), "etp").astype(jnp.float32),
        lax.psum(input_part.astype(jnp.bfloat16), "etp").astype(jnp.float32),
    )
    out_back, input_back = (
        lax.all_to_all(
            out_sum.astype(jnp.bfloat16), "expert", split_axis=0, concat_axis=0, tiled=True
        ),
        lax.all_to_all(
            input_sum.astype(jnp.bfloat16), "expert", split_axis=0, concat_axis=0, tiled=True
        ),
    )
    out_pairs = out_back.reshape(expert_count * capacity, features)[position].astype(jnp.float32)
    input_pairs = input_back.reshape(expert_count * capacity, features)[position].astype(
        jnp.float32
    )
    mixed = jnp.sum(combine_weights[:, :, None] * out_pairs, axis=1).astype(jnp.bfloat16)
    combine_grad = jnp.sum(grad_values[:, None, :] * out_pairs, axis=2)
    tokens_grad = jnp.sum(input_pairs, axis=1).astype(jnp.bfloat16)
    return (
        mixed,
        tokens_grad,
        combine_grad,
        gate_weight_grad[None],
        up_weight_grad[None],
        down_weight_grad[None],
    )


def solution(mesh):
    return jax.shard_map(
        shards,
        mesh=mesh,
        in_specs=(
            P("expert", None),
            P("expert", None),
            P("expert", None),
            P("expert", None),
            P("expert", None, "etp"),
            P("expert", None, "etp"),
            P("expert", "etp", None),
        ),
        out_specs=(
            P("expert", None),
            P("expert", None),
            P("expert", None),
            P("expert", None, "etp"),
            P("expert", None, "etp"),
            P("expert", "etp", None),
        ),
        check_vma=False,
    )
```

profile of v0, /device:TPU:97, one launch (start us, length us, event | category | flops | bytes accessed | tf_op | source)
XLA Modules:
  0.0 264.5 jit_solution(16705591363725790153)
XLA Ops:
  7.2 0.8 copy.30
  8.0 0.1 eq.29
  8.1 0.1 eq.25
  8.2 0.6 reduce-window.6
  8.8 0.2 slice_reduce_fusion
  9.1 0.1 fusion.20
  9.2 0.1 reshape.93
  9.3 0.1 copy.33
  9.4 0.7 compare_select_fusion.2
  10.1 0.1 copy.34
  10.2 0.1 reshape.94
  10.4 1.4 scatter_custom_fusion
  11.8 1.1 concatenate.6
  12.9 3.3 %gather_fusion = bf16[512,2048]{1,0:T(8,128)(2,1)} fusion(bf16[129,2048]{1,0:T(8,128)(2,1)S(1)} %concatenate.6, s32[1024]{0:T(1024)S(1)} %get-tuple-element.30), kind=kCustom, calls=%fused_computation | custom fusion | bytes 4196352 | tf_op jit(solution)/shard_map/gather | solution.py:64
  16.2 6.9 %all-to-all-start = ((bf16[16,32,2048]{2,1,0:T(8,128)(2,1)}), bf16[16,32,2048]{2,1,0:T(8,128)(2,1)}, u32[]{:S(2)}, u32[]{:S(2)}) async-start(bf16[16,32,2048]{2,1,0:T(8,128)(2,1)} %bitcast.2), calls=%async_computation | async-start | bytes 4194304 | tf_op jit(solution)/shard_map/all_to_all | solution.py:67
  23.1 0.0 copy-done.3
  23.1 0.1 copy.29
  23.2 0.1 mul.69
  23.4 0.0 copy-done
  23.4 1.0 mul.71
  24.4 2.4 mul.72
  26.9 1.8 multiply_convert_fusion
  28.6 0.1 concatenate.7
  28.8 3.3 %gather_fusion.2 = bf16[512,2048]{1,0:T(8,128)(2,1)} fusion(bf16[257,2048]{1,0:T(8,128)(2,1)S(1)} %concatenate.7, s32[1024]{0:T(1024)S(1)} %get-tuple-element.29), kind=kCustom, calls=%fused_computation.2 | custom fusion | bytes 4196352 | tf_op jit(solution)/shard_map/gather | solution.py:65
  32.1 21.6 %all-to-all-done = bf16[16,32,2048]{2,1,0:T(8,128)(2,1)} async-done(((bf16[16,32,2048]{2,1,0:T(8,128)(2,1)}), bf16[16,32,2048]{2,1,0:T(8,128)(2,1)}, u32[]{:S(2)}, u32[]{:S(2)}) %all-to-all-start) | async-done | bytes 2097184 | tf_op jit(solution)/shard_map/all_to_all | solution.py:67
  53.7 4.3 %all-to-all-start.2 = ((bf16[16,32,2048]{2,1,0:T(8,128)(2,1)}), bf16[16,32,2048]{2,1,0:T(8,128)(2,1)S(1)}, u32[]{:S(2)}, u32[]{:S(2)}) async-start(bf16[16,32,2048]{2,1,0:T(8,128)(2,1)} %bitcast.10), calls=%async_computation.2 | async-start | bytes 4194304 | tf_op jit(solution)/shard_map/all_to_all | solution.py:68
  57.9 0.2 all-reduce.5.cloned.1.call-start
  58.2 6.2 %fusion.6 = f32[512,896]{1,0:T(8,128)} fusion(bf16[512,2048]{1,0:T(8,128)(2,1)} %bitcast.3, bf16[1,2048,896]{2,1,0:T(8,128)(2,1)} %param.12), kind=kOutput, calls=%fused_computation.12 | convolution fusion | flops 1879048192 | bytes 7602176 | tf_op jit(solution)/shard_map/dot_general | solution.py:32
  64.4 22.3 %all-to-all-done.2 = bf16[16,32,2048]{2,1,0:T(8,128)(2,1)S(1)} async-done(((bf16[16,32,2048]{2,1,0:T(8,128)(2,1)}), bf16[16,32,2048]{2,1,0:T(8,128)(2,1)S(1)}, u32[]{:S(2)}, u32[]{:S(2)}) %all-to-all-start.2) | async-done | bytes 2097184 | tf_op jit(solution)/shard_map/all_to_all | solution.py:68
  86.7 5.2 %fusion.2 = f32[512,896]{1,0:T(8,128)S(1)} fusion(bf16[512,2048]{1,0:T(8,128)(2,1)S(1)} %bitcast.70, bf16[1,896,2048]{2,1,0:T(8,128)(2,1)} %param.13), kind=kOutput, calls=%fused_computation.8 | convolution fusion | flops 1879048192 | bytes 7602176 | tf_op jit(solution)/shard_map/dot_general | solution.py:19
  91.9 0.0 copy-done.1
  91.9 0.0 copy-done.6
  91.9 0.0 copy-done.12
  91.9 0.0 copy-start.4
  91.9 4.8 %multiply_convert_fusion.2 = (bf16[512,896]{1,0:T(8,128)(2,1)S(1)}, bf16[512,896]{1,0:T(8,128)(2,1)S(1)}, bf16[512,896]{1,0:T(8,128)(2,1)S(1)}) fusion(f32[512,896]{1,0:T(8,128)S(1)} %fusion.2, f32[512,896]{1,0:T(8,128)S(1)} %copy-done.12, bf16[512,2048]{1,0:T(8,128)(2,1)} %bitcast.3, bf16[1,2048,896]{2,1,0:T(8,128)(2,1)S(1)} %copy-done.6), kind=kOutput, calls=%fused_computation.26 | convolution fusion | flops 1885929472 | bytes 12189696 | tf_op jit(solution)/shard_map/dot_general | solution.py:31
  96.7 0.0 copy-start.9
  96.7 0.0 copy-start.7
  96.7 0.0 copy-start.10
  96.7 0.0 copy-done.4
  96.8 0.0 copy-start.5
  96.8 2.4 fusion.4
  99.2 0.6 copy-done.5
  99.8 3.7 %fusion.12 = bf16[16,32,2048]{2,1,0:T(8,128)(2,1)} fusion(bf16[16,32,896]{2,1,0:T(8,128)(2,1)S(1)} %bitcast.74, bf16[1,896,2048]{2,1,0:T(8,128)(2,1)S(1)} %copy-done.5), kind=kOutput, calls=%fused_computation.21 | convolution fusion | flops 1880096768 | bytes 6684672 | tf_op jit(solution)/shard_map/dot_general | solution.py:36
  103.4 3.7 %add_convert_fusion = bf16[512,2048]{1,0:T(8,128)(2,1)} fusion(f32[512,2048]{1,0:T(8,128)S(1)} %fusion.4, bf16[512,896]{1,0:T(8,128)(2,1)S(1)} %get-tuple-element.24, bf16[1,2048,896]{2,1,0:T(8,128)(2,1)S(1)} %copy-done.6), kind=kOutput, calls=%fused_computation.5 | convolution fusion | flops 1881145344 | bytes 10878976 | tf_op jit(solution)/shard_map/dot_general | solution.py:19
  107.1 0.0 all-reduce.5.cloned.1.call-update
  107.1 72.5 %all-reduce.5.cloned.1.call-done = (bf16[16,32,2048]{2,1,0:T(8,128)(2,1)}, bf16[16,32,2048]{2,1,0:T(8,128)(2,1)}) async-done(((bf16[16,32,2048]{2,1,0:T(8,128)(2,1)}, bf16[16,32,2048]{2,1,0:T(8,128)(2,1)}), (bf16[16,32,2048]{2,1,0:T(8,128)(2,1)}, bf16[16,32,2048]{2,1,0:T(8,128)(2,1)})) %all-reduce.5.cloned.1.call-update) | async-done | bytes 4194320 | tf_op jit(solution)/shard_map/psum | solution.py:79
  179.6 34.4 %all_to_all.20 = bf16[16,32,2048]{2,1,0:T(8,128)(2,1)} all-to-all(bf16[16,32,2048]{2,1,0:T(8,128)(2,1)} %get-tuple-element.20), channel_id=1, replica_groups=mesh['expert'=16,'etp'=8] {'expert'}, dimensions={0} | all-to-all | bytes 4194304 | tf_op jit(solution)/shard_map/all_to_all | solution.py:83
  214.0 3.9 %all-to-all-start.3 = ((bf16[16,32,2048]{2,1,0:T(8,128)(2,1)}), bf16[16,32,2048]{2,1,0:T(8,128)(2,1)S(1)}, u32[]{:S(2)}, u32[]{:S(2)}) async-start(bf16[16,32,2048]{2,1,0:T(8,128)(2,1)} %get-tuple-element.21), calls=%async_computation.3 | async-start | bytes 4194304 | tf_op jit(solution)/shard_map/all_to_all | solution.py:86
  217.9 1.2 convert_element_type.61
  219.1 0.1 copy.35
  219.2 0.1 reshape.111
  219.3 0.0 copy-start.11
  219.3 6.1 %convert_bitcast_fusion.1 = bf16[1,2048,896]{2,1,0:T(8,128)(2,1)} fusion(bf16[512,2048]{1,0:T(8,128)(2,1)} %bitcast.3, bf16[512,896]{1,0:T(8,128)(2,1)} %copy-done.9), kind=kOutput, calls=%fused_computation.19 | convolution fusion | flops 1880883200 | bytes 6684672 | tf_op jit(solution)/shard_map/dot_general | solution.py:25
  225.4 0.0 copy-done.11
  225.5 6.0 %convert_bitcast_fusion.2 = bf16[1,2048,896]{2,1,0:T(8,128)(2,1)} fusion(bf16[512,2048]{1,0:T(8,128)(2,1)} %bitcast.3, bf16[512,896]{1,0:T(8,128)(2,1)S(1)} %copy-done.11), kind=kOutput, calls=%fused_computation.20 | convolution fusion | flops 1880883200 | bytes 6684672 | tf_op jit(solution)/shard_map/dot_general | solution.py:25
  231.4 4.0 %convert_bitcast_fusion = bf16[1,896,2048]{2,1,0:T(8,128)(2,1)} fusion(bf16[512,896]{1,0:T(8,128)(2,1)S(1)} %copy-done.8, bf16[512,2048]{1,0:T(8,128)(2,1)S(1)} %bitcast.71), kind=kOutput, calls=%fused_computation.18 | convolution fusion | flops 1880883200 | bytes 6684672 | tf_op jit(solution)/shard_map/dot_general | solution.py:25
  235.4 4.2 %gather_fusion.1 = bf16[256,2048]{1,0:T(8,128)(2,1)S(1)} fusion(bf16[512,2048]{1,0:T(8,128)(2,1)} %bitcast.69, s32[1024]{0:T(1024)S(1)} %pad_clamp_fusion.1), kind=kCustom, calls=%fused_computation.1 | custom fusion | bytes 2098176 | tf_op jit(solution)/shard_map/gather | solution.py:90
  239.6 2.3 reshape.147
  241.9 6.5 %multiply_reduce_fusion = (f32[128,2]{1,0:T(8,128)S(1)}, bf16[128,2048]{1,0:T(8,128)(2,1)}) fusion(f32[128,2,2048]{2,1,0:T(2,128)} %reshape.147, f32[128,2048]{1,0:T(8,128)} %convert_element_type.61, f32[128,2]{1,0:T(8,128)S(1)} %copy.29), kind=kLoop, calls=%fused_computation.22 | loop fusion | flops 1834752 | bytes 3672064 | tf_op jit(solution)/shard_map/reduce_sum | solution.py:95
  248.5 0.6 copy.37
  249.1 2.8 %all-to-all-done.3 = bf16[16,32,2048]{2,1,0:T(8,128)(2,1)S(1)} async-done(((bf16[16,32,2048]{2,1,0:T(8,128)(2,1)}), bf16[16,32,2048]{2,1,0:T(8,128)(2,1)S(1)}, u32[]{:S(2)}, u32[]{:S(2)}) %all-to-all-start.3) | async-done | bytes 2097184 | tf_op jit(solution)/shard_map/all_to_all | solution.py:86
  251.9 1.4 gather_fusion.3
  253.3 0.7 reshape.130
  254.0 3.6 %reduce_sum.41 = bf16[128,2048]{1,0:T(8,128)(2,1)} reduce(bf16[128,2,2048]{2,1,0:T(2,128)(2,1)S(1)} %reshape.130, bf16[]{:T(256)} %constant.12.clone.1), dimensions={1}, to_apply=%region_7.8 | reduce | flops 262144 | bytes 1572866 | tf_op jit(solution)/shard_map/reduce_sum | solution.py:96
  (20 shorter events, 0.1 us)
Async XLA Ops:
  16.2 7.0 %copy-start.3 = (f32[128,2]{0,1:T(2,128)S(1)}, f32[128,2]{0,1:T(2,128)}, u32[]{:S(2)}) copy-start(f32[128,2]{0,1:T(2,128)} %param.10) | copy-start | bytes 3076
  16.2 7.2 %copy-start = (bf16[128,2048]{1,0:T(8,128)(2,1)S(1)}, bf16[128,2048]{1,0:T(8,128)(2,1)}, u32[]{:S(2)}) copy-start(bf16[128,2048]{1,0:T(8,128)(2,1)} %param.8) | copy-start | bytes 1572868
  16.2 37.5 %all-to-all-start = ((bf16[16,32,2048]{2,1,0:T(8,128)(2,1)}), bf16[16,32,2048]{2,1,0:T(8,128)(2,1)}, u32[]{:S(2)}, u32[]{:S(2)}) async-start(bf16[16,32,2048]{2,1,0:T(8,128)(2,1)} %bitcast.2), calls=%async_computation | async-start | bytes 4194304 | tf_op jit(solution)/shard_map/all_to_all | solution.py:67
  53.7 33.0 %all-to-all-start.2 = ((bf16[16,32,2048]{2,1,0:T(8,128)(2,1)}), bf16[16,32,2048]{2,1,0:T(8,128)(2,1)S(1)}, u32[]{:S(2)}, u32[]{:S(2)}) async-start(bf16[16,32,2048]{2,1,0:T(8,128)(2,1)} %bitcast.10), calls=%async_computation.2 | async-start | bytes 4194304 | tf_op jit(solution)/shard_map/all_to_all | solution.py:68
  57.9 121.7 %all-reduce.5.cloned.1.call-start = ((), (), s32[]{:S(2)}) async-start(), calls=%async_computation.4 | async-start | bytes 8388608 | tf_op jit(solution)/shard_map/psum | solution.py:79
  86.7 5.2 %copy-start.1 = (bf16[16,32,2048]{2,1,0:T(8,128)(2,1)}, bf16[16,32,2048]{2,1,0:T(8,128)(2,1)S(1)}, u32[]{:S(2)}) copy-start(bf16[16,32,2048]{2,1,0:T(8,128)(2,1)S(1)} %all-to-all-done.2) | copy-start | bytes 6291460
  86.7 5.2 %copy-start.6 = (bf16[1,2048,896]{2,1,0:T(8,128)(2,1)S(1)}, bf16[1,2048,896]{2,1,0:T(8,128)(2,1)}, u32[]{:S(2)}) copy-start(bf16[1,2048,896]{2,1,0:T(8,128)(2,1)} %param.11) | copy-start | bytes 11010052
  86.7 5.2 %copy-start.12 = (f32[512,896]{1,0:T(8,128)S(1)}, f32[512,896]{1,0:T(8,128)}, u32[]{:S(2)}) copy-start(f32[512,896]{1,0:T(8,128)} %fusion.6) | copy-start | bytes 5505028
  91.9 4.8 %copy-start.4 = (bf16[1,2048,896]{2,1,0:T(8,128)(2,1)S(1)}, bf16[1,2048,896]{2,1,0:T(8,128)(2,1)}, u32[]{:S(2)}) copy-start(bf16[1,2048,896]{2,1,0:T(8,128)(2,1)} %param.12) | copy-start | bytes 11010052
  96.7 2.4 copy-start.9
  96.7 2.4 copy-start.7
  96.7 6.7 %copy-start.10 = (bf16[512,896]{1,0:T(8,128)(2,1)}, bf16[512,896]{1,0:T(8,128)(2,1)S(1)}, u32[]{:S(2)}) copy-start(bf16[512,896]{1,0:T(8,128)(2,1)S(1)} %get-tuple-element.24) | copy-start | bytes 2752516
  96.8 3.0 %copy-start.5 = (bf16[1,896,2048]{2,1,0:T(8,128)(2,1)S(1)}, bf16[1,896,2048]{2,1,0:T(8,128)(2,1)}, u32[]{:S(2)}) copy-start(bf16[1,896,2048]{2,1,0:T(8,128)(2,1)} %param.13) | copy-start | bytes 11010052
  214.0 37.9 %all-to-all-start.3 = ((bf16[16,32,2048]{2,1,0:T(8,128)(2,1)}), bf16[16,32,2048]{2,1,0:T(8,128)(2,1)S(1)}, u32[]{:S(2)}, u32[]{:S(2)}) async-start(bf16[16,32,2048]{2,1,0:T(8,128)(2,1)} %get-tuple-element.21), calls=%async_computation.3 | async-start | bytes 4194304 | tf_op jit(solution)/shard_map/all_to_all | solution.py:86
  219.3 6.1 %copy-start.11 = (bf16[512,896]{1,0:T(8,128)(2,1)S(1)}, bf16[512,896]{1,0:T(8,128)(2,1)}, u32[]{:S(2)}) copy-start(bf16[512,896]{1,0:T(8,128)(2,1)} %copy-done.10) | copy-start | bytes 2752516
  225.4 6.0 %copy-start.2 = (bf16[16,32,2048]{2,1,0:T(8,128)(2,1)S(1)}, bf16[16,32,2048]{2,1,0:T(8,128)(2,1)}, u32[]{:S(2)}) copy-start(bf16[16,32,2048]{2,1,0:T(8,128)(2,1)} %copy-done.1) | copy-start | bytes 6291460
  225.5 6.0 %copy-start.8 = (bf16[512,896]{1,0:T(8,128)(2,1)S(1)}, bf16[512,896]{1,0:T(8,128)(2,1)}, u32[]{:S(2)}) copy-start(bf16[512,896]{1,0:T(8,128)(2,1)} %copy-done.7) | copy-start | bytes 2752516
Sparse Core Ops, SparseCore 0:
  107.3 72.3 all-reduce.4
where the time goes:
time: 265 us; the launch traced here: 264 us
  waiting for transfers between devices  119 us (45%)
  matrix products  42 us (16%)
  blocking collectives  34.4 us (13%)
  local copies, waits for them, and re-layouts  24.8 us (9%)
  starting transfers between devices  15.4 us (6%)
  other arithmetic  14.5 us (5%)
  between operations  14.3 us (5%)
    psum x1, waiting for transfers between devices, shards(): lax.psum(out_part.astype(jnp.bfloat16), 'etp').astype(jnp.float32)  72.5 us
    all_to_all x1, blocking collectives, shards(): lax.all_to_all(out_sum.astype(jnp.bfloat16), 'expert', split_axis=0, conc...  34.4 us
    all_to_all x1, waiting for transfers between devices, shards(): lax.all_to_all(send_grad, 'expert', split_axis=0, concat_axis=0, tiled=True)  22.3 us
    all_to_all x1, waiting for transfers between devices, shards(): lax.all_to_all(send_rows, 'expert', split_axis=0, concat_axis=0, tiled=True)  21.6 us
    dot_general x3, matrix products, contract_first(): lax.dot_general(left, right, (((0,), (0,)), ((), ())), preferred_element_...  16 us
    dot_general x3, matrix products, contract_last(): lax.dot_general(left, right, (((1,), (1,)), ((), ())), preferred_element_...  11.3 us
    all_to_all x1, starting transfers between devices, shards(): lax.all_to_all(send_rows, 'expert', split_axis=0, concat_axis=0, tiled=True)  6.94 us
    reduce_sum x1, other arithmetic, shards(): combine_grad = jnp.sum(grad_values[:, None, :] * out_pairs, axis=2)  6.54 us
  transfers between devices with their start and end apart: 4, of which 4 were waited for; matrix products, arithmetic and copies ran while one was open for 17% of the time, Pallas kernels for 0%

commit v1 on v0

--- a/solution.py
+++ b/solution.py
@@ -76,7 +76,7 @@
     input_part = input_part.reshape(expert_count, capacity, features)
     grad_values = out_grad.astype(jnp.float32)
     out_sum, input_sum = (
-        lax.psum(out_part.astype(jnp.bfloat16), "etp").astype(jnp.float32),
+        jnp.sum(lax.all_gather(out_part.astype(jnp.bfloat16), "etp"), axis=0).astype(jnp.float32),
         lax.psum(input_part.astype(jnp.bfloat16), "etp").astype(jnp.float32),
     )
     out_back, input_back = (

time: 265 us -> 332 us (1.25); the launches traced: 264 us -> 328 us
  waiting for transfers between devices: 119 us -> 197 us
  blocking collectives: 34.4 us -> 0 us
  other arithmetic: 14.5 us -> 24 us
  starting transfers between devices: 15.4 us -> 24.9 us
    all_gather x0 -> x1, waiting for transfers between devices: none -> 79.9 us  [shards(): lax.all_gather(out_part.astype(jnp.bfloat16), 'etp')]
    all_to_all x1 -> x0, blocking collectives: 34.4 us -> none  [shards(): lax.all_to_all(out_sum.astype(jnp.bfloat16), 'expert', split_axis=0, conc...]
    psum x1, waiting for transfers between devices: 72.5 us -> 60.5 us  [shards(): lax.psum(input_part.astype(jnp.bfloat16), 'etp').astype(jnp.float32)]
    reduce_sum x0 -> x1, other arithmetic: none -> 10.8 us  [shards(): jnp.sum(lax.all_gather(out_part.astype(jnp.bfloat16), 'etp'), axis=0)]
    all_to_all x0 -> x1, waiting for transfers between devices: none -> 9.27 us  [shards(): lax.all_to_all(out_sum.astype(jnp.bfloat16), 'expert', split_axis=0, conc...]
    all_to_all x0 -> x1, starting transfers between devices: none -> 6.96 us  [shards(): lax.all_to_all(out_sum.astype(jnp.bfloat16), 'expert', split_axis=0, conc...]
    all_to_all x1, waiting for transfers between devices: 22.3 us -> 26.1 us  [shards(): lax.all_to_all(send_grad, 'expert', split_axis=0, concat_axis=0, tiled=True)]
  transfers between devices with their start and end apart: 4 -> 6, of which waited for: 4 -> 5; matrix products, arithmetic and copies ran while one was open for 17% -> 15% of each run, Pallas kernels for 0% -> 0%
where the time goes in v1:
time: 332 us; the launch traced here: 328 us
  waiting for transfers between devices  197 us (59%)
  matrix products  43.4 us (13%)
  starting transfers between devices  24.9 us (8%)
  local copies, waits for them, and re-layouts  24.5 us (7%)
  other arithmetic  24 us (7%)
  between operations  14.4 us (4%)
    all_gather x1, waiting for transfers between devices, shards(): lax.all_gather(out_part.astype(jnp.bfloat16), 'etp')  79.9 us
    psum x1, waiting for transfers between devices, shards(): lax.psum(input_part.astype(jnp.bfloat16), 'etp').astype(jnp.float32)  60.5 us
    all_to_all x1, waiting for transfers between devices, shards(): lax.all_to_all(send_grad, 'expert', split_axis=0, concat_axis=0, tiled=True)  26.1 us
    all_to_all x1, waiting for transfers between devices, shards(): lax.all_to_all(send_rows, 'expert', split_axis=0, concat_axis=0, tiled=True)  20.9 us
    dot_general x3, matrix products, contract_first(): lax.dot_general(left, right, (((0,), (0,)), ((), ())), preferred_element_...  16 us
    dot_general x3, matrix products, contract_last(): lax.dot_general(left, right, (((1,), (1,)), ((), ())), preferred_element_...  11.7 us
    reduce_sum x1, other arithmetic, shards(): jnp.sum(lax.all_gather(out_part.astype(jnp.bfloat16), 'etp'), axis=0)  10.8 us
    all_to_all x1, waiting for transfers between devices, shards(): lax.all_to_all(out_sum.astype(jnp.bfloat16), 'expert', split_axis=0, conc...  9.27 us
  transfers between devices with their start and end apart: 6, of which 5 were waited for; matrix products, arithmetic and copies ran while one was open for 15% of the time, Pallas kernels for 0%

profile of v1, /device:TPU:97, one launch (start us, length us, event | category | flops | bytes accessed | tf_op | source)
XLA Modules:
  0.0 327.9 jit_solution(12014203662124627781)
XLA Ops:
  7.2 0.8 copy.30
  8.0 0.1 eq.25
  8.1 0.1 eq.29
  8.2 2.1 mul.71
  10.3 0.0 copy-start.4
  10.3 0.0 copy-start.3
  10.4 2.4 mul.72
  12.8 0.1 copy.29
  12.9 0.1 mul.69
  13.1 0.6 reduce-window.6
  13.7 0.2 slice_reduce_fusion
  13.9 0.1 fusion.20
  14.0 0.1 reshape.93
  14.1 0.1 copy.33
  14.2 0.1 copy.34
  14.3 0.1 reshape.94
  14.5 1.4 scatter_custom_fusion
  15.9 1.8 multiply_convert_fusion
  17.7 0.1 concatenate.7
  17.8 3.3 %gather_fusion.2 = bf16[512,2048]{1,0:T(8,128)(2,1)} fusion(bf16[257,2048]{1,0:T(8,128)(2,1)S(1)} %concatenate.7, s32[1024]{0:T(1024)S(1)} %get-tuple-element.27), kind=kCustom, calls=%fused_computation.2 | custom fusion | bytes 4196352 | tf_op jit(solution)/shard_map/gather | solution.py:65
  21.1 6.8 %all-to-all-start.2 = ((bf16[16,32,2048]{2,1,0:T(8,128)(2,1)}), bf16[16,32,2048]{2,1,0:T(8,128)(2,1)S(1)}, u32[]{:S(2)}, u32[]{:S(2)}) async-start(bf16[16,32,2048]{2,1,0:T(8,128)(2,1)} %bitcast.11), calls=%async_computation.2 | async-start | bytes 4194304 | tf_op jit(solution)/shard_map/all_to_all | solution.py:68
  27.9 1.1 concatenate.6
  29.0 3.3 %gather_fusion = bf16[512,2048]{1,0:T(8,128)(2,1)} fusion(bf16[129,2048]{1,0:T(8,128)(2,1)S(1)} %concatenate.6, s32[1024]{0:T(1024)S(1)} %get-tuple-element.28), kind=kCustom, calls=%fused_computation | custom fusion | bytes 4196352 | tf_op jit(solution)/shard_map/gather | solution.py:64
  32.2 26.1 %all-to-all-done.2 = bf16[16,32,2048]{2,1,0:T(8,128)(2,1)S(1)} async-done(((bf16[16,32,2048]{2,1,0:T(8,128)(2,1)}), bf16[16,32,2048]{2,1,0:T(8,128)(2,1)S(1)}, u32[]{:S(2)}, u32[]{:S(2)}) %all-to-all-start.2) | async-done | bytes 2097184 | tf_op jit(solution)/shard_map/all_to_all | solution.py:68
  58.4 4.4 %all-to-all-start = ((bf16[16,32,2048]{2,1,0:T(8,128)(2,1)}), bf16[16,32,2048]{2,1,0:T(8,128)(2,1)}, u32[]{:S(2)}, u32[]{:S(2)}) async-start(bf16[16,32,2048]{2,1,0:T(8,128)(2,1)} %bitcast.2), calls=%async_computation | async-start | bytes 4194304 | tf_op jit(solution)/shard_map/all_to_all | solution.py:67
  62.8 0.2 all-reduce.4.cloned.1.call-start
  63.1 5.6 %fusion.2 = f32[512,896]{1,0:T(8,128)} fusion(bf16[512,2048]{1,0:T(8,128)(2,1)S(1)} %bitcast.71, bf16[1,896,2048]{2,1,0:T(8,128)(2,1)} %param.13), kind=kOutput, calls=%fused_computation.8 | convolution fusion | flops 1879048192 | bytes 7602176 | tf_op jit(solution)/shard_map/dot_general | solution.py:19
  68.7 20.9 %all-to-all-done = bf16[16,32,2048]{2,1,0:T(8,128)(2,1)} async-done(((bf16[16,32,2048]{2,1,0:T(8,128)(2,1)}), bf16[16,32,2048]{2,1,0:T(8,128)(2,1)}, u32[]{:S(2)}, u32[]{:S(2)}) %all-to-all-start) | async-done | bytes 2097184 | tf_op jit(solution)/shard_map/all_to_all | solution.py:67
  89.5 5.1 %fusion.6 = f32[512,896]{1,0:T(8,128)S(1)} fusion(bf16[512,2048]{1,0:T(8,128)(2,1)} %bitcast.3, bf16[1,2048,896]{2,1,0:T(8,128)(2,1)} %param.12), kind=kOutput, calls=%fused_computation.12 | convolution fusion | flops 1879048192 | bytes 7602176 | tf_op jit(solution)/shard_map/dot_general | solution.py:32
  94.7 0.0 copy-start.5
  94.7 4.9 %multiply_convert_fusion.2 = (bf16[512,896]{1,0:T(8,128)(2,1)S(1)}, bf16[512,896]{1,0:T(8,128)(2,1)S(1)}, bf16[512,896]{1,0:T(8,128)(2,1)S(1)}) fusion(f32[512,896]{1,0:T(8,128)S(1)} %copy-done.11, f32[512,896]{1,0:T(8,128)S(1)} %fusion.6, bf16[512,2048]{1,0:T(8,128)(2,1)} %bitcast.3, bf16[1,2048,896]{2,1,0:T(8,128)(2,1)S(1)} %copy-done.6), kind=kOutput, calls=%fused_computation.26 | convolution fusion | flops 1885929472 | bytes 12189696 | tf_op jit(solution)/shard_map/dot_general | solution.py:31
  99.6 0.0 copy-start.9
  99.6 0.0 copy-start.12
  99.6 0.0 copy-start.7
  99.6 0.0 copy-done.5
  99.6 2.4 fusion.4
  102.0 3.7 %add_convert_fusion = bf16[512,2048]{1,0:T(8,128)(2,1)} fusion(f32[512,2048]{1,0:T(8,128)S(1)} %fusion.4, bf16[512,896]{1,0:T(8,128)(2,1)S(1)} %get-tuple-element.22, bf16[1,2048,896]{2,1,0:T(8,128)(2,1)S(1)} %copy-done.6), kind=kOutput, calls=%fused_computation.5 | convolution fusion | flops 1881145344 | bytes 10878976 | tf_op jit(solution)/shard_map/dot_general | solution.py:19
  105.7 0.0 all-reduce.4.cloned.1.call-update
  105.7 0.0 all-gather.3.cloned.1.call-start
  105.8 5.7 %fusion.12 = bf16[16,32,2048]{2,1,0:T(8,128)(2,1)} fusion(bf16[16,32,896]{2,1,0:T(8,128)(2,1)S(1)} %bitcast.75, bf16[1,896,2048]{2,1,0:T(8,128)(2,1)} %param.13), kind=kOutput, calls=%fused_computation.21 | convolution fusion | flops 1880096768 | bytes 6684672 | tf_op jit(solution)/shard_map/dot_general | solution.py:36
  111.5 0.0 all-gather.3.cloned.1.call-update
  111.5 60.5 %all-reduce.4.cloned.1.call-done = bf16[16,32,2048]{2,1,0:T(8,128)(2,1)} async-done(((bf16[16,32,2048]{2,1,0:T(8,128)(2,1)}), bf16[16,32,2048]{2,1,0:T(8,128)(2,1)}) %all-reduce.4.cloned.1.call-update) | async-done | bytes 2097168 | tf_op jit(solution)/shard_map/psum | solution.py:80
  172.0 6.5 %all-to-all-start.3 = ((bf16[16,32,2048]{2,1,0:T(8,128)(2,1)}), bf16[16,32,2048]{2,1,0:T(8,128)(2,1)S(1)}, u32[]{:S(2)}, u32[]{:S(2)}) async-start(bf16[16,32,2048]{2,1,0:T(8,128)(2,1)} %all-reduce.4.cloned.1.call-done), calls=%async_computation.3 | async-start | bytes 4194304 | tf_op jit(solution)/shard_map/all_to_all | solution.py:86
  178.5 79.9 %all-gather.3.cloned.1.call-done = bf16[128,32,2048]{2,1,0:T(8,128)(2,1)} async-done(((bf16[16,32,2048]{2,1,0:T(8,128)(2,1)}), bf16[128,32,2048]{2,1,0:T(8,128)(2,1)}) %all-gather.3.cloned.1.call-update) | async-done | bytes 16777232 | tf_op jit(solution)/shard_map/all_gather | solution.py:79
  258.5 10.8 %reduce_sum.52 = bf16[16,32,2048]{2,1,0:T(8,128)(2,1)} reduce(bf16[8,16,32,2048]{3,2,1,0:T(8,128)(2,1)} %bitcast.70, bf16[]{:T(256)} %constant.13.clone.1), dimensions={0}, to_apply=%region_4.5 | reduce | flops 7340032 | bytes 18874370 | tf_op jit(solution)/shard_map/reduce_sum | solution.py:79
  269.2 0.0 all-to-all-done.3
  269.2 7.0 %all-to-all-start.1 = ((bf16[16,32,2048]{2,1,0:T(8,128)(2,1)}), bf16[16,32,2048]{2,1,0:T(8,128)(2,1)}, u32[]{:S(2)}, u32[]{:S(2)}) async-start(bf16[16,32,2048]{2,1,0:T(8,128)(2,1)} %reduce_sum.52), calls=%async_computation.1 | async-start | bytes 4194304 | tf_op jit(solution)/shard_map/all_to_all | solution.py:83
  276.2 0.0 copy-done
  276.2 1.1 convert_element_type.63
  277.3 0.1 copy.35
  277.4 0.1 reshape.111
  277.6 0.0 copy-start.10
  277.6 6.1 %convert_bitcast_fusion.2 = bf16[1,2048,896]{2,1,0:T(8,128)(2,1)} fusion(bf16[512,2048]{1,0:T(8,128)(2,1)} %bitcast.3, bf16[512,896]{1,0:T(8,128)(2,1)} %copy-done.12), kind=kOutput, calls=%fused_computation.20 | convolution fusion | flops 1880883200 | bytes 6684672 | tf_op jit(solution)/shard_map/dot_general | solution.py:25
  283.7 0.0 copy-done.10
  283.7 6.0 %convert_bitcast_fusion.1 = bf16[1,2048,896]{2,1,0:T(8,128)(2,1)} fusion(bf16[512,2048]{1,0:T(8,128)(2,1)} %bitcast.3, bf16[512,896]{1,0:T(8,128)(2,1)S(1)} %copy-done.10), kind=kOutput, calls=%fused_computation.19 | convolution fusion | flops 1880883200 | bytes 6684672 | tf_op jit(solution)/shard_map/dot_general | solution.py:25
  289.7 4.0 %convert_bitcast_fusion = bf16[1,896,2048]{2,1,0:T(8,128)(2,1)} fusion(bf16[512,896]{1,0:T(8,128)(2,1)S(1)} %copy-done.8, bf16[512,2048]{1,0:T(8,128)(2,1)S(1)} %bitcast.72), kind=kOutput, calls=%fused_computation.18 | convolution fusion | flops 1880883200 | bytes 6684672 | tf_op jit(solution)/shard_map/dot_general | solution.py:25
  293.6 1.4 gather_fusion.3
  295.0 1.0 reshape.130
  296.0 3.6 %reduce_sum.54 = bf16[128,2048]{1,0:T(8,128)(2,1)} reduce(bf16[128,2,2048]{2,1,0:T(2,128)(2,1)S(1)} %reshape.130, bf16[]{:T(256)} %constant.13.clone.1), dimensions={1}, to_apply=%region_7.8 | reduce | flops 262144 | bytes 1572866 | tf_op jit(solution)/shard_map/reduce_sum | solution.py:96
  299.6 9.3 %all-to-all-done.1 = bf16[16,32,2048]{2,1,0:T(8,128)(2,1)} async-done(((bf16[16,32,2048]{2,1,0:T(8,128)(2,1)}), bf16[16,32,2048]{2,1,0:T(8,128)(2,1)}, u32[]{:S(2)}, u32[]{:S(2)}) %all-to-all-start.1) | async-done | bytes 2097184 | tf_op jit(solution)/shard_map/all_to_all | solution.py:83
  308.9 4.2 %gather_fusion.1 = bf16[256,2048]{1,0:T(8,128)(2,1)S(1)} fusion(bf16[512,2048]{1,0:T(8,128)(2,1)} %bitcast.10, s32[1024]{0:T(1024)S(1)} %pad_clamp_fusion.1), kind=kCustom, calls=%fused_computation.1 | custom fusion | bytes 2098176 | tf_op jit(solution)/shard_map/gather | solution.py:90
  313.1 1.3 reshape.148
  314.5 6.0 %multiply_reduce_fusion = (f32[128,2]{1,0:T(8,128)S(1)}, bf16[128,2048]{1,0:T(8,128)(2,1)}) fusion(f32[128,2,2048]{2,1,0:T(2,128)S(1)} %reshape.148, f32[128,2048]{1,0:T(8,128)} %convert_element_type.63, f32[128,2]{1,0:T(8,128)S(1)} %copy.29), kind=kLoop, calls=%fused_computation.22 | loop fusion | flops 1834752 | bytes 3672064 | tf_op jit(solution)/shard_map/reduce_sum | solution.py:95
  320.4 0.6 copy.37
  (25 shorter events, 0.1 us)
Async XLA Ops:
  10.3 2.5 copy-start.4
  10.3 3.8 %copy-start.3 = (s32[128,2]{0,1:T(2,128)S(1)}, s32[128,2]{0,1:T(2,128)}, u32[]{:S(2)}) copy-start(s32[128,2]{0,1:T(2,128)} %param.9) | copy-start | bytes 3076
  21.1 37.3 %all-to-all-start.2 = ((bf16[16,32,2048]{2,1,0:T(8,128)(2,1)}), bf16[16,32,2048]{2,1,0:T(8,128)(2,1)S(1)}, u32[]{:S(2)}, u32[]{:S(2)}) async-start(bf16[16,32,2048]{2,1,0:T(8,128)(2,1)} %bitcast.11), calls=%async_computation.2 | async-start | bytes 4194304 | tf_op jit(solution)/shard_map/all_to_all | solution.py:68
  58.4 4.7 %copy-start.1 = (bf16[16,32,2048]{2,1,0:T(8,128)(2,1)}, bf16[16,32,2048]{2,1,0:T(8,128)(2,1)S(1)}, u32[]{:S(2)}) copy-start(bf16[16,32,2048]{2,1,0:T(8,128)(2,1)S(1)} %all-to-all-done.2) | copy-start | bytes 6291460
  58.4 31.2 %all-to-all-start = ((bf16[16,32,2048]{2,1,0:T(8,128)(2,1)}), bf16[16,32,2048]{2,1,0:T(8,128)(2,1)}, u32[]{:S(2)}, u32[]{:S(2)}) async-start(bf16[16,32,2048]{2,1,0:T(8,128)(2,1)} %bitcast.2), calls=%async_computation | async-start | bytes 4194304 | tf_op jit(solution)/shard_map/all_to_all | solution.py:67
  62.8 109.2 %all-reduce.4.cloned.1.call-start = ((), (), s32[]{:S(2)}) async-start(), calls=%async_computation.4 | async-start | bytes 4194304 | tf_op jit(solution)/shard_map/psum | solution.py:80
  89.5 5.2 %copy-start.6 = (bf16[1,2048,896]{2,1,0:T(8,128)(2,1)S(1)}, bf16[1,2048,896]{2,1,0:T(8,128)(2,1)}, u32[]{:S(2)}) copy-start(bf16[1,2048,896]{2,1,0:T(8,128)(2,1)} %param.11) | copy-start | bytes 11010052
  89.5 5.2 %copy-start.11 = (f32[512,896]{1,0:T(8,128)S(1)}, f32[512,896]{1,0:T(8,128)}, u32[]{:S(2)}) copy-start(f32[512,896]{1,0:T(8,128)} %fusion.2) | copy-start | bytes 5505028
  94.7 4.9 %copy-start.5 = (bf16[1,2048,896]{2,1,0:T(8,128)(2,1)S(1)}, bf16[1,2048,896]{2,1,0:T(8,128)(2,1)}, u32[]{:S(2)}) copy-start(bf16[1,2048,896]{2,1,0:T(8,128)(2,1)} %param.12) | copy-start | bytes 11010052
  99.6 2.4 copy-start.9
  99.6 2.4 copy-start.12
  99.6 6.2 %copy-start.7 = (bf16[512,896]{1,0:T(8,128)(2,1)}, bf16[512,896]{1,0:T(8,128)(2,1)S(1)}, u32[]{:S(2)}) copy-start(bf16[512,896]{1,0:T(8,128)(2,1)S(1)} %get-tuple-element.24) | copy-start | bytes 2752516
  105.7 152.7 %all-gather.3.cloned.1.call-start = ((), (), s32[]{:S(2)}) async-start(), calls=%async_computation.5 | async-start | bytes 18874368 | tf_op jit(solution)/shard_map/all_gather | solution.py:79
  172.0 97.2 %all-to-all-start.3 = ((bf16[16,32,2048]{2,1,0:T(8,128)(2,1)}), bf16[16,32,2048]{2,1,0:T(8,128)(2,1)S(1)}, u32[]{:S(2)}, u32[]{:S(2)}) async-start(bf16[16,32,2048]{2,1,0:T(8,128)(2,1)} %all-reduce.4.cloned.1.call-done), calls=%async_computation.3 | async-start | bytes 4194304 | tf_op jit(solution)/shard_map/all_to_all | solution.py:86
  269.2 7.0 %copy-start = (bf16[128,2048]{1,0:T(8,128)(2,1)S(1)}, bf16[128,2048]{1,0:T(8,128)(2,1)}, u32[]{:S(2)}) copy-start(bf16[128,2048]{1,0:T(8,128)(2,1)} %param.8) | copy-start | bytes 1572868
  269.2 39.7 %all-to-all-start.1 = ((bf16[16,32,2048]{2,1,0:T(8,128)(2,1)}), bf16[16,32,2048]{2,1,0:T(8,128)(2,1)}, u32[]{:S(2)}, u32[]{:S(2)}) async-start(bf16[16,32,2048]{2,1,0:T(8,128)(2,1)} %reduce_sum.52), calls=%async_computation.1 | async-start | bytes 4194304 | tf_op jit(solution)/shard_map/all_to_all | solution.py:83
  277.6 6.1 %copy-start.10 = (bf16[512,896]{1,0:T(8,128)(2,1)S(1)}, bf16[512,896]{1,0:T(8,128)(2,1)}, u32[]{:S(2)}) copy-start(bf16[512,896]{1,0:T(8,128)(2,1)} %copy-done.9) | copy-start | bytes 2752516
  283.7 6.0 %copy-start.2 = (bf16[16,32,2048]{2,1,0:T(8,128)(2,1)S(1)}, bf16[16,32,2048]{2,1,0:T(8,128)(2,1)}, u32[]{:S(2)}) copy-start(bf16[16,32,2048]{2,1,0:T(8,128)(2,1)} %copy-done.1) | copy-start | bytes 6291460
  283.7 6.0 %copy-start.8 = (bf16[512,896]{1,0:T(8,128)(2,1)S(1)}, bf16[512,896]{1,0:T(8,128)(2,1)}, u32[]{:S(2)}) copy-start(bf16[512,896]{1,0:T(8,128)(2,1)} %copy-done.7) | copy-start | bytes 2752516
Sparse Core Ops, SparseCore 0:
  105.9 66.1 all-reduce.3
  174.3 84.1 all-gather.2
